TPU v7x, 512 devices: a whole 4x8x8 slice. The times are simulated.
512 devices in a mesh: head: 8 (over y), blk: 64 (over z, x, core).
Axes of the slice: x: 4, y: 8, z: 8, core: 2. Of those that a mesh axis runs over, the one named last changes fastest.
Arguments:
- inputs: bfloat16 [4, 64, 7168], P(None, None, 'blk'), may hold values from -40 to 40
- ln_gain: bfloat16 [7168], P('blk'), may hold values from 0.099609375 to 1.8984375
- ln_bias: bfloat16 [7168], P('blk'), may hold values from -3 to 3
- w_query: bfloat16 [7168, 7168], P('blk', 'head'), may hold values from -0.0625 to 0.0625
- w_key: bfloat16 [7168, 7168], P('blk', 'head'), may hold values from -0.0625 to 0.0625
- w_value: bfloat16 [7168, 7168], P('blk', 'head'), may hold values from -0.0625 to 0.0625
- b_query: bfloat16 [7168], P('head'), may hold values from -3 to 3
- b_key: bfloat16 [7168], P('head'), may hold values from -4 to 4
- b_value: bfloat16 [7168], P('head'), may hold values from -3 to 3
- w_out: bfloat16 [7168, 7168], P('head', 'blk'), may hold values from -0.5 to 0.5
- b_out: bfloat16 [7168], P('blk'), may hold values from -3 to 3
- prefix_keys: bfloat16 [1536, 16, 7168], P('blk', None, 'head'), may hold values from -110 to 110
- prefix_values: bfloat16 [1536, 16, 7168], P('blk', None, 'head'), may hold values from -6 to 6
- suffix_keys: bfloat16 [64, 256, 7168], P('blk', None, 'head'), may hold values from -110 to 110
- suffix_values: bfloat16 [64, 256, 7168], P('blk', None, 'head'), may hold values from -6 to 6
- page_table: int32 [8, 288], replicated, may hold values from 0 to 1535, as said below
- prompt_len: int32 [8], replicated, may hold values from 1 to 4608, as said below
- gen_len: int32 [8], replicated, may hold values from 1 to 252, as said below
- parents: int32 [4, 64], replicated, may hold values from 0 to 63, as said below
Outputs:
- hidden: bfloat16 [4, 64, 7168], P(None, None, 'blk')
- final_keys: bfloat16 [64, 256, 7168], P('blk', None, 'head')
- final_values: bfloat16 [64, 256, 7168], P('blk', None, 'head')
Inputs may be any that keep to these rules, and one draw needn't show every extreme that they name: `page_table`: the first ceil(prompt_len[r] / 16) entries of row r are distinct pages that no other request lists; later entries are 0 and hold no tokens of r. `prompt_len`: the longest request has exactly 4608 tokens. `gen_len`: some request has exactly 252. parents[s, b] is a beam of the same request as b.
All inputs are finite; a program needn't handle non-finite values.
Results may differ from a plain program's by a relative error of at most 0.0065.
The roundings to bfloat16 on the way count: a program that leaves them out, or rounds other values in their place, can miss the bound.
Values may be sent and summed in bfloat16 or wider, within the bound.
No kernel may reach another device: no remote copies, remote signals or barrier semaphores. Data moves between devices by JAX's collectives and lax.ppermute only.
A program may use at most 128 MiB of HBM per device.

v0:
```python
import math
import jax
import jax.numpy as jnp
import numpy as np
from jax import lax
from jax.sharding import Mesh
from jax.sharding import PartitionSpec as P

D = 7168
HEAD_DIM = 128
BEAMS = 8
PAGE = 16
GEN = 256
STEPS = 4
MASKED = -1e30
NORM_EPSILON = 1e-05
BLK_PARTS = ("z", "x", "core")
GROUP = ("x", "core")


def nested(reduce, value):
    for axis in reversed(BLK_PARTS):
        value = reduce(value, axis)
    return value


def blk_index():
    index = lax.axis_index("z")
    for axis in BLK_PARTS[1:]:
        index = index * lax.axis_size(axis) + lax.axis_index(axis)
    return index


def body(
    inputs,
    ln_gain,
    ln_bias,
    w_query,
    w_key,
    w_value,
    b_query,
    b_key,
    b_value,
    w_out,
    b_out,
    prefix_keys,
    prefix_values,
    suffix_keys,
    suffix_values,
    page_table,
    prompt_len,
    gen_len,
    parents,
):
    blocks = 1
    for axis in BLK_PARTS:
        blocks *= lax.axis_size(axis)
    me = blk_index()
    steps = inputs.shape[0]
    batch = inputs.shape[1]
    feat_here = w_query.shape[1]
    heads_here = feat_here // HEAD_DIM
    pages_here = prefix_keys.shape[0]
    requests = page_table.shape[0]
    slot_count = page_table.shape[1]
    rows = steps * batch
    score_scale = 1.0 / math.sqrt(HEAD_DIM)
    my_request = me // BEAMS
    first_beam = my_request * BEAMS
    my_gen = gen_len[my_request]
    beam_ids = jnp.arange(batch, dtype=jnp.int32)
    anc = {}
    for s in range(steps):
        x = beam_ids
        anc[s, s] = x
        for t in range(s, -1, -1):
            x = jnp.take(parents[t], x)
            anc[t - 1, s] = x
    origin = jnp.stack([anc[-1, s] for s in range(steps)])
    rows_in = inputs.astype(jnp.float32).reshape(rows, -1)
    stats = jnp.stack([jnp.sum(rows_in, axis=1), jnp.sum(rows_in * rows_in, axis=1)], axis=1)
    stats = nested(lax.psum, stats)
    row_mean = stats[:, 0] / D
    variance = stats[:, 1] / D - row_mean * row_mean
    normed = (
        (rows_in - row_mean[:, None])
        * lax.rsqrt(variance + NORM_EPSILON)[:, None]
        * ln_gain.astype(jnp.float32)
        + ln_bias.astype(jnp.float32)
    ).astype(jnp.bfloat16)
    weights_all = jnp.concatenate([w_query, w_key, w_value], axis=1)
    bias_all = jnp.concatenate([b_query, b_key, b_value]).astype(jnp.float32)
    partial = jnp.dot(normed, weights_all, preferred_element_type=jnp.float32)
    projected = (nested(lax.psum, partial) + bias_all[None, :]).astype(jnp.bfloat16)
    queries = projected[:, :feat_here].reshape(steps, batch, heads_here, HEAD_DIM)
    key_new = projected[:, feat_here : 2 * feat_here].reshape(steps, batch, feat_here)
    value_new = projected[:, 2 * feat_here :].reshape(steps, batch, feat_here)
    beam_request = beam_ids // BEAMS
    beam_prompt = jnp.take(prompt_len, beam_request)
    page_ids = me * pages_here + jnp.arange(pages_here, dtype=jnp.int32)
    slot_ids = jnp.arange(slot_count, dtype=jnp.int32)
    slot_live = slot_ids[None, :] * PAGE < prompt_len[:, None]
    page_match = (
        (page_table[:, :, None] == page_ids[None, None, :]) & slot_live[:, :, None]
    ).astype(jnp.int32)
    request_ids = jnp.arange(requests, dtype=jnp.int32)
    page_request = jnp.sum(page_match * request_ids[:, None, None], axis=(0, 1))
    page_slot = jnp.sum(page_match * slot_ids[None, :, None], axis=(0, 1))
    page_used = jnp.sum(page_match, axis=(0, 1)) > 0
    token_pos = (page_slot[:, None] * PAGE + jnp.arange(PAGE, dtype=jnp.int32)[None, :]).reshape(-1)
    token_request = jnp.repeat(page_request, PAGE)
    token_used = jnp.repeat(page_used, PAGE)
    prefix_live = (
        token_used[None, :]
        & (token_request[None, :] == beam_request[:, None])
        & (token_pos[None, :] < beam_prompt[:, None])
    )
    page_keys = prefix_keys.reshape(pages_here * PAGE, heads_here, HEAD_DIM)
    page_values = prefix_values.reshape(pages_here * PAGE, heads_here, HEAD_DIM)
    flat_queries = queries.reshape(rows, heads_here, HEAD_DIM)
    prompt_scores = (
        jnp.einsum("rhd,thd->rht", flat_queries, page_keys, preferred_element_type=jnp.float32)
        * score_scale
    ).reshape(steps, batch, heads_here, -1)
    prompt_live = prefix_live[None, :, None, :]
    prompt_top = jnp.max(jnp.where(prompt_live, prompt_scores, MASKED), axis=3)
    group_queries = lax.dynamic_slice_in_dim(queries, first_beam, BEAMS, axis=1)
    group_origin = lax.dynamic_slice_in_dim(origin, first_beam, BEAMS, axis=1)
    own_keys = suffix_keys[0].reshape(GEN, heads_here, HEAD_DIM)
    own_values = suffix_values[0].reshape(GEN, heads_here, HEAD_DIM)
    cache_scores = (
        jnp.einsum("sbhd,jhd->sbhj", group_queries, own_keys, preferred_element_type=jnp.float32)
        * score_scale
    )
    gen_rows = jnp.arange(GEN, dtype=jnp.int32)
    cache_live = (group_origin == me)[:, :, None, None] & (gen_rows < my_gen)[None, None, None, :]
    cache_top = jnp.max(jnp.where(cache_live, cache_scores, MASKED), axis=3)
    own_beam = me
    own_queries = lax.dynamic_index_in_dim(queries, own_beam, axis=1, keepdims=False)
    new_src = jnp.stack(
        [
            jnp.stack([anc[t, s][own_beam] if t <= s else own_beam for t in range(steps)])
            for s in range(steps)
        ]
    )
    step_ids = jnp.arange(steps, dtype=jnp.int32)
    new_keys_here = key_new[step_ids[None, :], new_src].reshape(steps, steps, heads_here, HEAD_DIM)
    new_values_here = value_new[step_ids[None, :], new_src].reshape(
        steps, steps, heads_here, HEAD_DIM
    )
    new_scores = (
        jnp.einsum("shd,sthd->sht", own_queries, new_keys_here, preferred_element_type=jnp.float32)
        * score_scale
    )
    new_live = (step_ids[None, :] <= step_ids[:, None])[:, None, :]
    new_top = jnp.max(jnp.where(new_live, new_scores, MASKED), axis=2)
    local_top = prompt_top
    group_top = jnp.maximum(
        lax.dynamic_slice_in_dim(local_top, first_beam, BEAMS, axis=1), cache_top
    )
    local_top = lax.dynamic_update_slice_in_dim(local_top, group_top, first_beam, axis=1)
    own_top = jnp.maximum(
        lax.dynamic_index_in_dim(local_top, own_beam, axis=1, keepdims=True), new_top[:, None]
    )
    local_top = lax.dynamic_update_slice_in_dim(local_top, own_top, own_beam, axis=1)
    top = nested(lax.pmax, local_top)
    prompt_weights = jnp.where(
        prompt_live, jnp.exp(prompt_scores - top[:, :, :, None]), 0.0
    ).astype(jnp.bfloat16)
    weighted = jnp.einsum(
        "rht,thd->rhd",
        prompt_weights.reshape(rows, heads_here, -1),
        page_values,
        preferred_element_type=jnp.float32,
    ).reshape(steps, batch, heads_here, HEAD_DIM)
    totals = jnp.sum(prompt_weights.astype(jnp.float32), axis=3)
    group_top_all = lax.dynamic_slice_in_dim(top, first_beam, BEAMS, axis=1)
    cache_weights = jnp.where(
        cache_live, jnp.exp(cache_scores - group_top_all[:, :, :, None]), 0.0
    ).astype(jnp.bfloat16)
    cache_weighted = jnp.einsum(
        "sbhj,jhd->sbhd", cache_weights, own_values, preferred_element_type=jnp.float32
    )
    cache_totals = jnp.sum(cache_weights.astype(jnp.float32), axis=3)
    own_top_all = lax.dynamic_index_in_dim(top, own_beam, axis=1, keepdims=False)
    new_weights = jnp.where(new_live, jnp.exp(new_scores - own_top_all[:, :, None]), 0.0).astype(
        jnp.bfloat16
    )
    new_weighted = jnp.einsum(
        "sht,sthd->shd", new_weights, new_values_here, preferred_element_type=jnp.float32
    )
    new_totals = jnp.sum(new_weights.astype(jnp.float32), axis=2)
    group_weighted = lax.dynamic_slice_in_dim(weighted, first_beam, BEAMS, axis=1) + cache_weighted
    weighted = lax.dynamic_update_slice_in_dim(weighted, group_weighted, first_beam, axis=1)
    group_totals = lax.dynamic_slice_in_dim(totals, first_beam, BEAMS, axis=1) + cache_totals
    totals = lax.dynamic_update_slice_in_dim(totals, group_totals, first_beam, axis=1)
    own_weighted = (
        lax.dynamic_index_in_dim(weighted, own_beam, axis=1, keepdims=True) + new_weighted[:, None]
    )
    weighted = lax.dynamic_update_slice_in_dim(weighted, own_weighted, own_beam, axis=1)
    own_totals = (
        lax.dynamic_index_in_dim(totals, own_beam, axis=1, keepdims=True) + new_totals[:, None]
    )
    totals = lax.dynamic_update_slice_in_dim(totals, own_totals, own_beam, axis=1)
    lanes = 128
    packed = jnp.concatenate(
        [
            weighted.reshape(rows, feat_here),
            jnp.pad(totals.reshape(rows, heads_here), ((0, 0), (0, lanes - heads_here))),
        ],
        axis=1,
    )
    packed = nested(lax.psum, packed)
    weighted = packed[:, :feat_here].reshape(rows, heads_here, HEAD_DIM)
    totals = packed[:, feat_here : feat_here + heads_here]
    attention = (weighted / totals[:, :, None]).reshape(rows, feat_here).astype(jnp.bfloat16)
    head_terms = jnp.dot(attention, w_out, preferred_element_type=jnp.float32)
    head_total = lax.psum(head_terms, "head")
    hidden = (head_total + b_out.astype(jnp.float32)[None, :]).astype(jnp.bfloat16)
    hidden = hidden.reshape(steps, batch, -1)
    final_origin = origin[steps - 1]
    pick = lax.dynamic_slice_in_dim(final_origin, first_beam, BEAMS) - first_beam
    my_final_src = [anc[t, steps - 1][own_beam] for t in range(steps)]
    write_rows = my_gen + step_ids

    def reorder(cache, fresh):
        chunks = cache[0].reshape(BEAMS, GEN // BEAMS, feat_here)
        spread = lax.all_to_all(chunks, GROUP, 0, 0, tiled=True)
        picked = jnp.take(spread, pick, axis=0)
        back = lax.all_to_all(picked, GROUP, 0, 0, tiled=True).reshape(GEN, feat_here)
        new_rows = jnp.stack([fresh[t, my_final_src[t]] for t in range(steps)])
        hit = gen_rows[:, None] == write_rows[None, :]
        chosen = jnp.argmax(hit, axis=1)
        out = jnp.where(jnp.any(hit, axis=1)[:, None], jnp.take(new_rows, chosen, axis=0), back)
        return out[None]

    final_keys = reorder(suffix_keys, key_new)
    final_values = reorder(suffix_values, value_new)
    return (hidden, final_keys, final_values)


def solution(mesh):
    heads = mesh.shape["head"]
    blocks = mesh.shape["blk"]
    cores = 2
    group_chips = BEAMS // cores
    devices = np.asarray(mesh.devices).reshape(heads, blocks // BEAMS, group_chips, cores)
    fine = Mesh(devices, ("head",) + BLK_PARTS)
    blk = BLK_PARTS
    in_specs = (
        P(None, None, blk),
        P(blk),
        P(blk),
        P(blk, "head"),
        P(blk, "head"),
        P(blk, "head"),
        P("head"),
        P("head"),
        P("head"),
        P("head", blk),
        P(blk),
        P(blk, None, "head"),
        P(blk, None, "head"),
        P(blk, None, "head"),
        P(blk, None, "head"),
        P(),
        P(),
        P(),
        P(),
    )
    out_specs = (P(None, None, blk), P(blk, None, "head"), P(blk, None, "head"))
    return jax.shard_map(body, mesh=fine, in_specs=in_specs, out_specs=out_specs, check_vma=False)
```

profile of v0, /device:TPU:2, one launch (start us, length us, event | category | flops | bytes accessed | tf_op | source)
XLA Modules:
  0.0 610.5 jit_solution(4780817149313871015)
XLA Ops:
  9.7 2.5 psum.70
  12.2 13.6 %psum.71 = f32[256,2]{0,1:T(2,128)S(1)} all-reduce(f32[256,2]{0,1:T(2,128)S(1)} %psum.70), channel_id=1, replica_groups=mesh['head'=8,'z'=8,'x'=4,'core'=2] {'x'}, use_global_device_ids=true, to_apply=%region_6.7 | all-reduce | flops 512 | bytes 4096 | tf_op jit(solution)/shard_map/psum | solution.py:23
  25.8 18.2 %psum.72 = f32[256,2]{0,1:T(2,128)S(1)} all-reduce(f32[256,2]{0,1:T(2,128)S(1)} %psum.71), channel_id=1, replica_groups=mesh['head'=8,'z'=8,'x'=4,'core'=2] {'z'}, use_global_device_ids=true, to_apply=%region_7.8 | all-reduce | flops 512 | bytes 4096 | tf_op jit(solution)/shard_map/psum | solution.py:23
  44.9 3.2 fusion.12
  48.2 35.7 %all-reduce.9.cloned.1.call-done = f32[256,2688]{1,0:T(8,128)} async-done(((f32[256,2688]{1,0:T(8,128)}), f32[256,2688]{1,0:T(8,128)}) %all-reduce.9.cloned.1.call-update) | async-done | bytes 2752528 | tf_op jit(solution)/shard_map/psum | solution.py:23
  84.9 1.7 reshape.492
  92.2 74.5 %all-reduce.11.cloned.1.call-done = f32[256,2688]{1,0:T(8,128)} async-done(((f32[256,2688]{1,0:T(8,128)}), f32[256,2688]{1,0:T(8,128)}) %all-reduce.11.cloned.1.call-update) | async-done | bytes 2752528 | tf_op jit(solution)/shard_map/psum | solution.py:23
  169.2 2.0 copy.51
  174.7 1.9 add_bitcast_fusion.3
  180.3 2.0 copy.55
  184.5 5.1 and_select_fusion.7
  189.8 73.7 %all-reduce.13.cloned.1.call-done = f32[256,2688]{1,0:T(8,128)} async-done(((f32[256,2688]{1,0:T(8,128)}), f32[256,2688]{1,0:T(8,128)}) %all-reduce.13.cloned.1.call-update) | async-done | bytes 2752528 | tf_op jit(solution)/shard_map/psum | solution.py:23
  263.5 1.9 add_convert_fusion
  268.1 2.1 fusion
  271.8 1.7 gather_fusion
  274.7 3.3 pmax.21
  278.0 13.9 %pmax.22 = f32[4,64,7]{1,0,2:T(4,128)S(1)} all-reduce(f32[4,64,7]{1,0,2:T(4,128)S(1)} %pmax.21), channel_id=1, replica_groups=mesh['head'=8,'z'=8,'x'=4,'core'=2] {'x'}, use_global_device_ids=true, to_apply=%region_15.17 | all-reduce | flops 1792 | bytes 14336 | tf_op jit(solution)/shard_map/pmax | solution.py:23
  291.9 30.1 %pmax.23 = f32[4,64,7]{1,0,2:T(4,128)S(1)} all-reduce(f32[4,64,7]{1,0,2:T(4,128)S(1)} %pmax.22), channel_id=1, replica_groups=mesh['head'=8,'z'=8,'x'=4,'core'=2] {'z'}, use_global_device_ids=true, to_apply=%region_16.18 | all-reduce | flops 1792 | bytes 14336 | tf_op jit(solution)/shard_map/pmax | solution.py:23
  325.1 2.9 fusion.8
  328.1 1.7 gather_fusion.1
  330.1 2.0 fusion.6
  334.6 1.7 copy.58
  337.7 36.2 %all-reduce.15.cloned.1.call-done = f32[256,1024]{1,0:T(8,128)} async-done(((f32[256,1024]{1,0:T(8,128)}), f32[256,1024]{1,0:T(8,128)}) %all-reduce.15.cloned.1.call-update) | async-done | bytes 1048592 | tf_op jit(solution)/shard_map/psum | solution.py:23
  374.0 4.9 all-to-all-start.2
  387.1 4.8 all-to-all-start
  392.0 44.4 %all-reduce.17.cloned.1.call-done = f32[256,1024]{1,0:T(8,128)} async-done(((f32[256,1024]{1,0:T(8,128)}), f32[256,1024]{1,0:T(8,128)}) %all-reduce.17.cloned.1.call-update) | async-done | bytes 1048592 | tf_op jit(solution)/shard_map/psum | solution.py:23
  438.8 4.8 all-to-all-start.3
  445.2 6.6 %all-to-all-done.3 = bf16[8,32,896]{2,1,0:T(8,128)(2,1)S(1)} async-done(((bf16[8,32,896]{2,1,0:T(8,128)(2,1)}), bf16[8,32,896]{2,1,0:T(8,128)(2,1)S(1)}, u32[]{:S(2)}, u32[]{:S(2)}) %all-to-all-start.3) | async-done | bytes 458784 | tf_op jit(solution)/shard_map/all_to_all | solution.py:230
  451.8 4.8 all-to-all-start.1
  459.1 63.0 %all-reduce.19.cloned.1.call-done = f32[256,1024]{1,0:T(8,128)} async-done(((f32[256,1024]{1,0:T(8,128)}), f32[256,1024]{1,0:T(8,128)}) %all-reduce.19.cloned.1.call-update) | async-done | bytes 1048592 | tf_op jit(solution)/shard_map/psum | solution.py:23
  524.4 2.4 fusion.18
  528.1 73.9 %all-reduce.21.cloned.1.call-done = f32[256,112]{0,1:T(8,128)} async-done(((f32[256,112]{0,1:T(8,128)}), f32[256,112]{0,1:T(8,128)}) %all-reduce.21.cloned.1.call-update) | async-done | bytes 114704 | tf_op jit(solution)/shard_map/psum | solution.py:218
  (170 shorter events, 49.3 us)
Async XLA Ops:
  7.2 517.2 %copy-start = (bf16[896,112]{0,1:T(8,128)(2,1)S(1)}, bf16[896,112]{0,1:T(8,128)(2,1)}, u32[]{:S(2)}) copy-start(bf16[896,112]{0,1:T(8,128)(2,1)} %param.34) | copy-start | bytes 602116
  7.2 76.7 %all-reduce.9.cloned.1.call-start = ((), (), s32[]{:S(2)}) async-start(), calls=%async_computation.4 | async-start | bytes 5505024 | tf_op jit(solution)/shard_map/psum | solution.py:23
  48.1 35.9 %copy-start.3 = (s32[8]{0:T(128)S(1)}, s32[8]{0:T(128)}, u32[]{:S(2)}) copy-start(s32[8]{0:T(128)} %param.41) | copy-start | bytes 100
  48.1 36.0 %copy-start.4 = (s32[8,288]{1,0:T(8,128)S(1)}, s32[8,288]{1,0:T(8,128)}, u32[]{:S(2)}) copy-start(s32[8,288]{1,0:T(8,128)} %param.40) | copy-start | bytes 27652
  48.1 36.8 %copy-start.1 = (bf16[24,16,896]{2,1,0:T(8,128)(2,1)S(1)}, bf16[24,16,896]{2,1,0:T(8,128)(2,1)}, u32[]{:S(2)}) copy-start(bf16[24,16,896]{2,1,0:T(8,128)(2,1)} %param.36) | copy-start | bytes 2064388
  48.2 38.5 %copy-start.8 = (s32[4,64]{1,0:T(4,128)S(1)}, s32[4,64]{1,0:T(4,128)}, u32[]{:S(2)}) copy-start(s32[4,64]{1,0:T(4,128)} %param.43) | copy-start | bytes 3076
  48.2 118.5 %all-reduce.11.cloned.1.call-start = ((), (), s32[]{:S(2)}) async-start(), calls=%async_computation.5 | async-start | bytes 5505024 | tf_op jit(solution)/shard_map/psum | solution.py:23
  83.9 179.6 %all-reduce.13.cloned.1.call-start = ((), (), s32[]{:S(2)}) async-start(), calls=%async_computation.6 | async-start | bytes 5505024 | tf_op jit(solution)/shard_map/psum | solution.py:23
  92.2 86.5 %copy-start.2 = (bf16[24,16,896]{2,1,0:T(8,128)(2,1)S(1)}, bf16[24,16,896]{2,1,0:T(8,128)(2,1)}, u32[]{:S(2)}) copy-start(bf16[24,16,896]{2,1,0:T(8,128)(2,1)} %param.37) | copy-start | bytes 2064388
  166.7 15.6 %copy-start.9 = (s32[8]{0:T(128)S(1)}, s32[8]{0:T(128)}, u32[]{:S(2)}) copy-start(s32[8]{0:T(128)} %param.42) | copy-start | bytes 100
  166.7 22.8 %copy-start.5 = (bf16[896]{0:T(1024)(128)(2,1)S(1)}, bf16[896]{0:T(1024)(128)(2,1)}, u32[]{:S(2)}) copy-start(bf16[896]{0:T(1024)(128)(2,1)} %param.33) | copy-start | bytes 5380
  166.7 22.8 %copy-start.6 = (bf16[896]{0:T(1024)(128)(2,1)S(1)}, bf16[896]{0:T(1024)(128)(2,1)}, u32[]{:S(2)}) copy-start(bf16[896]{0:T(1024)(128)(2,1)} %param.32) | copy-start | bytes 5380
  166.7 22.8 %copy-start.7 = (bf16[896]{0:T(1024)(128)(2,1)S(1)}, bf16[896]{0:T(1024)(128)(2,1)}, u32[]{:S(2)}) copy-start(bf16[896]{0:T(1024)(128)(2,1)} %param.31) | copy-start | bytes 5380
  166.7 207.2 %all-reduce.15.cloned.1.call-start = ((), (), s32[]{:S(2)}) async-start(), calls=%async_computation.7 | async-start | bytes 2097152 | tf_op jit(solution)/shard_map/psum | solution.py:23
  336.5 46.0 %copy-start.10 = (bf16[112]{0:T(256)(128)(2,1)S(1)}, bf16[112]{0:T(256)(128)(2,1)}, u32[]{:S(2)}) copy-start(bf16[112]{0:T(256)(128)(2,1)} %param.35) | copy-start | bytes 676
  337.7 98.7 %all-reduce.17.cloned.1.call-start = ((), (), s32[]{:S(2)}) async-start(), calls=%async_computation.8 | async-start | bytes 2097152 | tf_op jit(solution)/shard_map/psum | solution.py:23
  374.0 13.2 %all-to-all-start.2 = ((bf16[8,32,896]{2,1,0:T(8,128)(2,1)}), bf16[8,32,896]{2,1,0:T(8,128)(2,1)S(1)}, u32[]{:S(2)}, u32[]{:S(2)}) async-start(bf16[8,32,896]{2,1,0:T(8,128)(2,1)} %bitcast.68), calls=%async_computation.2 | async-start | bytes 917504 | tf_op jit(solution)/shard_map/all_to_all | solution.py:228
  387.1 49.9 %all-to-all-start = ((bf16[8,32,896]{2,1,0:T(8,128)(2,1)}), bf16[8,32,896]{2,1,0:T(8,128)(2,1)S(1)}, u32[]{:S(2)}, u32[]{:S(2)}) async-start(bf16[8,32,896]{2,1,0:T(8,128)(2,1)} %bitcast.61), calls=%async_computation | async-start | bytes 917504 | tf_op jit(solution)/shard_map/all_to_all | solution.py:228
  392.0 130.1 %all-reduce.19.cloned.1.call-start = ((), (), s32[]{:S(2)}) async-start(), calls=%async_computation.9 | async-start | bytes 2097152 | tf_op jit(solution)/shard_map/psum | solution.py:23
  438.8 13.0 %all-to-all-start.3 = ((bf16[8,32,896]{2,1,0:T(8,128)(2,1)}), bf16[8,32,896]{2,1,0:T(8,128)(2,1)S(1)}, u32[]{:S(2)}, u32[]{:S(2)}) async-start(bf16[8,32,896]{2,1,0:T(8,128)(2,1)} %get-tuple-element.45), calls=%async_computation.3 | async-start | bytes 917504 | tf_op jit(solution)/shard_map/all_to_all | solution.py:230
  451.8 75.1 %all-to-all-start.1 = ((bf16[8,32,896]{2,1,0:T(8,128)(2,1)}), bf16[8,32,896]{2,1,0:T(8,128)(2,1)S(1)}, u32[]{:S(2)}, u32[]{:S(2)}) async-start(bf16[8,32,896]{2,1,0:T(8,128)(2,1)} %get-tuple-element.46), calls=%async_computation.1 | async-start | bytes 917504 | tf_op jit(solution)/shard_map/all_to_all | solution.py:230
  456.6 145.4 %all-reduce.21.cloned.1.call-start = ((), (), s32[]{:S(2)}) async-start(), calls=%async_computation.10 | async-start | bytes 229376 | tf_op jit(solution)/shard_map/psum | solution.py:218
Sparse Core Ops, SparseCore 0:
  48.3 35.5 all-reduce.8
  86.4 80.2 all-reduce.10
  169.2 94.2 all-reduce.12
  337.8 36.1 all-reduce.14
  376.3 60.0 all-reduce.16
  438.6 83.4 all-reduce.18
  527.0 74.9 all-reduce.20
where the time goes:
time: 612 us; the launch traced here: 611 us
  waiting for transfers between devices  409 us (67%)
  blocking collectives  81.5 us (13%)
  local copies, waits for them, and re-layouts  41.3 us (7%)
  other arithmetic  24.4 us (4%)
  between operations  20.1 us (3%)
  starting transfers between devices  19.6 us (3%)
  matrix products  14.2 us (2%)
    psum x6, waiting for transfers between devices, nested(): value = reduce(value, axis)  328 us
    psum x1, waiting for transfers between devices, body(): head_total = lax.psum(head_terms, 'head')  73.9 us
    pmax x3, blocking collectives, nested(): value = reduce(value, axis)  47.3 us
    psum x3, blocking collectives, nested(): value = reduce(value, axis)  34.2 us
  transfers between devices with their start and end apart: 11, of which 9 were waited for; matrix products, arithmetic and copies ran while one was open for 7% of the time, Pallas kernels for 0%

commit v1 on v0

--- a/solution.py
+++ b/solution.py
@@ -215,7 +215,7 @@
     totals = packed[:, feat_here : feat_here + heads_here]
     attention = (weighted / totals[:, :, None]).reshape(rows, feat_here).astype(jnp.bfloat16)
     head_terms = jnp.dot(attention, w_out, preferred_element_type=jnp.float32)
-    head_total = lax.psum(head_terms, "head")
+    head_total = jnp.sum(lax.all_gather(head_terms, "head"), axis=0)
     hidden = (head_total + b_out.astype(jnp.float32)[None, :]).astype(jnp.bfloat16)
     hidden = hidden.reshape(steps, batch, -1)
     final_origin = origin[steps - 1]

time: 612 us -> 561 us (0.917)
  waiting for transfers between devices: 409 us -> 332 us
  blocking collectives: 81.5 us -> 109 us
    psum x1 -> x0, waiting for transfers between devices: 73.9 us -> none  [body(): head_total = lax.psum(head_terms, 'head')]
    all_gather x0 -> x1, blocking collectives: none -> 27.5 us  [body(): head_total = jnp.sum(lax.all_gather(head_terms, 'head'), axis=0)]
    psum x6, waiting for transfers between devices: 328 us -> 321 us  [nested(): value = reduce(value, axis)]
  transfers between devices with their start and end apart: 11 -> 10, of which waited for: 9 -> 8; matrix products, arithmetic and copies ran while one was open for 7% -> 7% of each run, Pallas kernels for 0% -> 0%
where the time goes in v1:
time: 561 us; the launch traced here: 560 us
  waiting for transfers between devices  332 us (59%)
  blocking collectives  109 us (19%)
  local copies, waits for them, and re-layouts  40.2 us (7%)
  other arithmetic  24.4 us (4%)
  starting transfers between devices  21.1 us (4%)
  between operations  20.3 us (4%)
  matrix products  12.1 us (2%)
    psum x6, waiting for transfers between devices, nested(): value = reduce(value, axis)  321 us
    pmax x3, blocking collectives, nested(): value = reduce(value, axis)  47.3 us
    psum x3, blocking collectives, nested(): value = reduce(value, axis)  34.2 us
    all_gather x1, blocking collectives, body(): head_total = jnp.sum(lax.all_gather(head_terms, 'head'), axis=0)  27.5 us
    all_to_all x2, starting transfers between devices, reorder(): spread = lax.all_to_all(chunks, GROUP, 0, 0, tiled=True)  11.4 us
  transfers between devices with their start and end apart: 10, of which 8 were waited for; matrix products, arithmetic and copies ran while one was open for 7% of the time, Pallas kernels for 0%

profile of v1, /device:TPU:2, one launch (start us, length us, event | category | flops | bytes accessed | tf_op | source)
XLA Modules:
  0.0 559.5 jit_solution(11922454372975548873)
XLA Ops:
  9.7 2.5 psum.63
  12.2 13.6 %psum.64 = f32[256,2]{0,1:T(2,128)S(1)} all-reduce(f32[256,2]{0,1:T(2,128)S(1)} %psum.63), channel_id=1, replica_groups=mesh['head'=8,'z'=8,'x'=4,'core'=2] {'x'}, use_global_device_ids=true, to_apply=%region_6.7 | all-reduce | flops 512 | bytes 4096 | tf_op jit(solution)/shard_map/psum | solution.py:23
  25.8 18.2 %psum.65 = f32[256,2]{0,1:T(2,128)S(1)} all-reduce(f32[256,2]{0,1:T(2,128)S(1)} %psum.64), channel_id=1, replica_groups=mesh['head'=8,'z'=8,'x'=4,'core'=2] {'z'}, use_global_device_ids=true, to_apply=%region_7.8 | all-reduce | flops 512 | bytes 4096 | tf_op jit(solution)/shard_map/psum | solution.py:23
  44.9 3.2 fusion.12
  48.2 35.7 %all-reduce.8.cloned.1.call-done = f32[256,2688]{1,0:T(8,128)} async-done(((f32[256,2688]{1,0:T(8,128)}), f32[256,2688]{1,0:T(8,128)}) %all-reduce.8.cloned.1.call-update) | async-done | bytes 2752528 | tf_op jit(solution)/shard_map/psum | solution.py:23
  84.9 1.7 reshape.496
  92.2 74.5 %all-reduce.10.cloned.1.call-done = f32[256,2688]{1,0:T(8,128)} async-done(((f32[256,2688]{1,0:T(8,128)}), f32[256,2688]{1,0:T(8,128)}) %all-reduce.10.cloned.1.call-update) | async-done | bytes 2752528 | tf_op jit(solution)/shard_map/psum | solution.py:23
  169.2 2.0 copy.83
  174.8 1.9 add_bitcast_fusion.3
  180.6 2.0 copy.87
  184.6 5.1 and_select_fusion.7
  190.0 73.6 %all-reduce.12.cloned.1.call-done = f32[256,2688]{1,0:T(8,128)} async-done(((f32[256,2688]{1,0:T(8,128)}), f32[256,2688]{1,0:T(8,128)}) %all-reduce.12.cloned.1.call-update) | async-done | bytes 2752528 | tf_op jit(solution)/shard_map/psum | solution.py:23
  263.5 1.9 add_convert_fusion
  268.1 2.1 fusion
  271.8 1.7 gather_fusion
  274.7 3.3 pmax.21
  278.0 13.9 %pmax.22 = f32[4,64,7]{1,0,2:T(4,128)S(1)} all-reduce(f32[4,64,7]{1,0,2:T(4,128)S(1)} %pmax.21), channel_id=1, replica_groups=mesh['head'=8,'z'=8,'x'=4,'core'=2] {'x'}, use_global_device_ids=true, to_apply=%region_15.17 | all-reduce | flops 1792 | bytes 14336 | tf_op jit(solution)/shard_map/pmax | solution.py:23
  291.9 30.1 %pmax.23 = f32[4,64,7]{1,0,2:T(4,128)S(1)} all-reduce(f32[4,64,7]{1,0,2:T(4,128)S(1)} %pmax.22), channel_id=1, replica_groups=mesh['head'=8,'z'=8,'x'=4,'core'=2] {'z'}, use_global_device_ids=true, to_apply=%region_16.18 | all-reduce | flops 1792 | bytes 14336 | tf_op jit(solution)/shard_map/pmax | solution.py:23
  325.1 2.9 fusion.8
  328.1 1.7 gather_fusion.1
  330.1 2.0 fusion.6
  334.6 1.7 copy.90
  337.7 6.4 %all-to-all-start.2 = ((bf16[8,32,896]{2,1,0:T(8,128)(2,1)}), bf16[8,32,896]{2,1,0:T(8,128)(2,1)S(1)}, u32[]{:S(2)}, u32[]{:S(2)}) async-start(bf16[8,32,896]{2,1,0:T(8,128)(2,1)} %bitcast.68), calls=%async_computation.2 | async-start | bytes 917504 | tf_op jit(solution)/shard_map/all_to_all | solution.py:228
  349.8 24.2 %all-reduce.14.cloned.1.call-done = f32[256,1024]{1,0:T(8,128)} async-done(((f32[256,1024]{1,0:T(8,128)}), f32[256,1024]{1,0:T(8,128)}) %all-reduce.14.cloned.1.call-update) | async-done | bytes 1048592 | tf_op jit(solution)/shard_map/psum | solution.py:23
  374.7 4.9 all-to-all-start
  380.9 7.0 %all-to-all-done = bf16[8,32,896]{2,1,0:T(8,128)(2,1)S(1)} async-done(((bf16[8,32,896]{2,1,0:T(8,128)(2,1)}), bf16[8,32,896]{2,1,0:T(8,128)(2,1)S(1)}, u32[]{:S(2)}, u32[]{:S(2)}) %all-to-all-start) | async-done | bytes 458784 | tf_op jit(solution)/shard_map/all_to_all | solution.py:228
  389.6 4.8 all-to-all-start.3
  394.5 41.9 %all-reduce.16.cloned.1.call-done = f32[256,1024]{1,0:T(8,128)} async-done(((f32[256,1024]{1,0:T(8,128)}), f32[256,1024]{1,0:T(8,128)}) %all-reduce.16.cloned.1.call-update) | async-done | bytes 1048592 | tf_op jit(solution)/shard_map/psum | solution.py:23
  436.4 4.8 all-to-all-start.1
  445.3 4.1 all-to-all-done.1
  450.7 71.4 %all-reduce.18.cloned.1.call-done = f32[256,1024]{1,0:T(8,128)} async-done(((f32[256,1024]{1,0:T(8,128)}), f32[256,1024]{1,0:T(8,128)}) %all-reduce.18.cloned.1.call-update) | async-done | bytes 1048592 | tf_op jit(solution)/shard_map/psum | solution.py:23
  523.9 27.5 %all-gather = f32[2048,112]{0,1:T(8,128)S(1)} all-gather(f32[256,112]{0,1:T(8,128)S(1)} %fusion.18), channel_id=2, replica_groups=mesh['head'=8,'z'=8,'x'=4,'core'=2] {'head'}, dimensions={0}, use_global_device_ids=true | all-gather | bytes 1032192 | tf_op jit(solution)/shard_map/all_gather | solution.py:218
  (172 shorter events, 47.0 us)
Async XLA Ops:
  7.2 516.4 %copy-start = (bf16[896,112]{0,1:T(8,128)(2,1)S(1)}, bf16[896,112]{0,1:T(8,128)(2,1)}, u32[]{:S(2)}) copy-start(bf16[896,112]{0,1:T(8,128)(2,1)} %param.34) | copy-start | bytes 602116
  7.2 76.7 %all-reduce.8.cloned.1.call-start = ((), (), s32[]{:S(2)}) async-start(), calls=%async_computation.4 | async-start | bytes 5505024 | tf_op jit(solution)/shard_map/psum | solution.py:23
  48.1 35.9 %copy-start.3 = (s32[8]{0:T(128)S(1)}, s32[8]{0:T(128)}, u32[]{:S(2)}) copy-start(s32[8]{0:T(128)} %param.41) | copy-start | bytes 100
  48.1 36.0 %copy-start.5 = (s32[8,288]{1,0:T(8,128)S(1)}, s32[8,288]{1,0:T(8,128)}, u32[]{:S(2)}) copy-start(s32[8,288]{1,0:T(8,128)} %param.40) | copy-start | bytes 27652
  48.1 36.8 %copy-start.1 = (bf16[24,16,896]{2,1,0:T(8,128)(2,1)S(1)}, bf16[24,16,896]{2,1,0:T(8,128)(2,1)}, u32[]{:S(2)}) copy-start(bf16[24,16,896]{2,1,0:T(8,128)(2,1)} %param.36) | copy-start | bytes 2064388
  48.2 38.5 %copy-start.9 = (s32[4,64]{1,0:T(4,128)S(1)}, s32[4,64]{1,0:T(4,128)}, u32[]{:S(2)}) copy-start(s32[4,64]{1,0:T(4,128)} %param.43) | copy-start | bytes 3076
  48.2 118.5 %all-reduce.10.cloned.1.call-start = ((), (), s32[]{:S(2)}) async-start(), calls=%async_computation.5 | async-start | bytes 5505024 | tf_op jit(solution)/shard_map/psum | solution.py:23
  83.9 179.6 %all-reduce.12.cloned.1.call-start = ((), (), s32[]{:S(2)}) async-start(), calls=%async_computation.6 | async-start | bytes 5505024 | tf_op jit(solution)/shard_map/psum | solution.py:23
  92.2 86.7 %copy-start.2 = (bf16[24,16,896]{2,1,0:T(8,128)(2,1)S(1)}, bf16[24,16,896]{2,1,0:T(8,128)(2,1)}, u32[]{:S(2)}) copy-start(bf16[24,16,896]{2,1,0:T(8,128)(2,1)} %param.37) | copy-start | bytes 2064388
  166.7 15.8 %copy-start.10 = (s32[8]{0:T(128)S(1)}, s32[8]{0:T(128)}, u32[]{:S(2)}) copy-start(s32[8]{0:T(128)} %param.42) | copy-start | bytes 100
  166.7 23.0 %copy-start.6 = (bf16[896]{0:T(1024)(128)(2,1)S(1)}, bf16[896]{0:T(1024)(128)(2,1)}, u32[]{:S(2)}) copy-start(bf16[896]{0:T(1024)(128)(2,1)} %param.33) | copy-start | bytes 5380
  166.7 23.0 %copy-start.7 = (bf16[896]{0:T(1024)(128)(2,1)S(1)}, bf16[896]{0:T(1024)(128)(2,1)}, u32[]{:S(2)}) copy-start(bf16[896]{0:T(1024)(128)(2,1)} %param.32) | copy-start | bytes 5380
  166.7 23.0 %copy-start.8 = (bf16[896]{0:T(1024)(128)(2,1)S(1)}, bf16[896]{0:T(1024)(128)(2,1)}, u32[]{:S(2)}) copy-start(bf16[896]{0:T(1024)(128)(2,1)} %param.31) | copy-start | bytes 5380
  166.7 207.2 %all-reduce.14.cloned.1.call-start = ((), (), s32[]{:S(2)}) async-start(), calls=%async_computation.7 | async-start | bytes 2097152 | tf_op jit(solution)/shard_map/psum | solution.py:23
  336.3 11.5 %copy-start.11 = (bf16[112]{0:T(256)(128)(2,1)S(1)}, bf16[112]{0:T(256)(128)(2,1)}, u32[]{:S(2)}) copy-start(bf16[112]{0:T(256)(128)(2,1)} %param.35) | copy-start | bytes 676
  337.7 37.0 %all-to-all-start.2 = ((bf16[8,32,896]{2,1,0:T(8,128)(2,1)}), bf16[8,32,896]{2,1,0:T(8,128)(2,1)S(1)}, u32[]{:S(2)}, u32[]{:S(2)}) async-start(bf16[8,32,896]{2,1,0:T(8,128)(2,1)} %bitcast.68), calls=%async_computation.2 | async-start | bytes 917504 | tf_op jit(solution)/shard_map/all_to_all | solution.py:228
  344.1 92.3 %all-reduce.16.cloned.1.call-start = ((), (), s32[]{:S(2)}) async-start(), calls=%async_computation.8 | async-start | bytes 2097152 | tf_op jit(solution)/shard_map/psum | solution.py:23
  374.7 13.2 %all-to-all-start = ((bf16[8,32,896]{2,1,0:T(8,128)(2,1)}), bf16[8,32,896]{2,1,0:T(8,128)(2,1)S(1)}, u32[]{:S(2)}, u32[]{:S(2)}) async-start(bf16[8,32,896]{2,1,0:T(8,128)(2,1)} %bitcast.61), calls=%async_computation | async-start | bytes 917504 | tf_op jit(solution)/shard_map/all_to_all | solution.py:228
  389.6 46.9 %all-to-all-start.3 = ((bf16[8,32,896]{2,1,0:T(8,128)(2,1)}), bf16[8,32,896]{2,1,0:T(8,128)(2,1)S(1)}, u32[]{:S(2)}, u32[]{:S(2)}) async-start(bf16[8,32,896]{2,1,0:T(8,128)(2,1)} %get-tuple-element.42), calls=%async_computation.3 | async-start | bytes 917504 | tf_op jit(solution)/shard_map/all_to_all | solution.py:230
  394.4 127.7 %all-reduce.18.cloned.1.call-start = ((), (), s32[]{:S(2)}) async-start(), calls=%async_computation.9 | async-start | bytes 2097152 | tf_op jit(solution)/shard_map/psum | solution.py:23
  436.4 13.0 %all-to-all-start.1 = ((bf16[8,32,896]{2,1,0:T(8,128)(2,1)}), bf16[8,32,896]{2,1,0:T(8,128)(2,1)S(1)}, u32[]{:S(2)}, u32[]{:S(2)}) async-start(bf16[8,32,896]{2,1,0:T(8,128)(2,1)} %get-tuple-element.43), calls=%async_computation.1 | async-start | bytes 917504 | tf_op jit(solution)/shard_map/all_to_all | solution.py:230
  522.1 1.5 copy-start.4
Sparse Core Ops, SparseCore 0:
  48.3 35.5 all-reduce.7
  86.4 80.2 all-reduce.9
  169.2 94.2 all-reduce.11
  337.8 36.1 all-reduce.13
  376.3 60.0 all-reduce.15
  438.6 83.4 all-reduce.17
